TPU v7x, 256 devices: a whole 4x4x8 slice. The times are simulated.
256 devices in a mesh: kv: 8 (over z), blk: 32 (over y, x, core).
Axes of the slice: x: 4, y: 4, z: 8, core: 2. Of those that a mesh axis runs over, the one named last changes fastest.
Arguments:
- embeds: bfloat16 [1, 256, 3072], P(None, None, 'blk'), may hold values from -40 to 40
- attn_norm: float32 [3072], P('blk'), may hold values from 0.25 to 1.75
- query_key_value_weight: bfloat16 [3072, 5120], P('blk', 'kv'), may hold values from -0.109375 to 0.109375
- w_out: bfloat16 [3072, 3072], P('kv', 'blk'), may hold values from -0.109375 to 0.109375
- mlp_norm: float32 [3072], P('blk'), may hold values from 0.25 to 1.75
- w_gate: bfloat16 [3072, 8192], P('blk', 'kv'), may hold values from -0.109375 to 0.109375
- w_up: bfloat16 [3072, 8192], P('blk', 'kv'), may hold values from -0.109375 to 0.109375
- w_down: bfloat16 [8192, 3072], P('kv', 'blk'), may hold values from -0.0625 to 0.0625
- prompt_key_slots: bfloat16 [256, 8, 128, 128], P('blk', 'kv'), may hold values from -210 to 210
- prompt_value_slots: bfloat16 [256, 8, 128, 128], P('blk', 'kv'), may hold values from -6 to 6
- generated_keys: bfloat16 [256, 8, 127, 128], P('blk', 'kv'), may hold values from -10 to 10
- generated_values: bfloat16 [256, 8, 127, 128], P('blk', 'kv'), may hold values from -6 to 6
- parents: int32 [1, 256], P(None, 'blk'), may hold values from 0 to 7
- prompt_length: int32 [32], replicated, may hold values from 1024 to 8192
- tenant_bounds: int32 [5], replicated, may hold values from 0 to 32, as said below
- slot_table: int32 [256], P('blk'), may hold values from 0 to 256, as said below
Outputs:
- hidden_out: float32 [1, 256, 3072], P(None, None, 'blk')
- keys_out: bfloat16 [256, 8, 128, 128], P('blk', 'kv')
- values_out: bfloat16 [256, 8, 128, 128], P('blk', 'kv')
Inputs may be any that keep to these rules, and one draw needn't show every extreme that they name: parents[s, b] is the beam, among the 8 beams of b's request, whose cache beam b continues at step s. tenant_bounds[0] = 0 and tenant_bounds[4] = 32, strictly rising. `slot_table`: with L_t the largest prompt_length of tenant t's requests, every block j below ceil(L_t / 128) of every tenant t stands in exactly one slot as t * 64 + j, no other block stands anywhere, and 256 marks an empty slot.
All inputs are finite; a program needn't handle non-finite values.
Results may differ from a plain program's by a relative error of at most 0.012.
The roundings to bfloat16 on the way count: a program that leaves them out, or rounds other values in their place, can miss the bound.
Values may be sent and summed in bfloat16 or wider, within the bound.
No kernel may reach another device: no remote copies, remote signals or barrier semaphores. Data moves between devices by JAX's collectives and lax.ppermute only.
A program may use at most 64 MiB of HBM per device.

v0:
```python
import math
import jax
import jax.numpy as jnp
from jax import lax
from jax.sharding import PartitionSpec as P

MODEL_WIDTH = 3072
QUERY_HEADS = 24
KEY_VALUE_HEADS = 8
HEAD_WIDTH = 128
REQUEST_BEAMS = 8
TENANT_COUNT = 4
BLOCK_POSITIONS = 128
PROMPT_BLOCKS = 64
EARLIER_TOKENS = 127
DECODE_STEPS = 1
masked_score = -1e30


def exchange(value, axis, bit):
    count = lax.axis_size(axis)
    return lax.ppermute(value, axis, [(i, i ^ 1 << bit) for i in range(count)])


def butterfly_sum(value, axis):
    count = lax.axis_size(axis)
    if count & count - 1:
        return lax.psum(value, axis)
    for bit in range(count.bit_length() - 1):
        value = value + exchange(value, axis, bit)
    return value


def scatter_sum(value, axis):
    count = lax.axis_size(axis)
    pieces = value.reshape((count, value.shape[0] // count) + value.shape[1:])
    return jnp.sum(lax.all_to_all(pieces, axis, 0, 0, tiled=False), axis=0)


def rotate(values, angles):
    half = values.shape[-1] // 2
    first = values[..., :half]
    second = values[..., half:]
    cosine = jnp.cos(angles)
    sine = jnp.sin(angles)
    return jnp.concatenate(
        [first * cosine - second * sine, second * cosine + first * sine], axis=-1
    )


def angles_for(positions, head_size):
    half = head_size // 2
    freq = jnp.exp(jnp.arange(half, dtype=jnp.float32) * (-math.log(500000.0) / half))
    return positions.astype(jnp.float32)[:, None] * freq[None, :]


def across_heads(partial_value):
    return butterfly_sum(partial_value, "kv")


def body(
    embeds,
    attn_norm,
    query_key_value_weight,
    w_out,
    mlp_norm,
    w_gate,
    w_up,
    w_down,
    prompt_key_slots,
    prompt_value_slots,
    generated_keys,
    generated_values,
    parents,
    prompt_length,
    tenant_bounds,
    slot_table,
):
    blocks = lax.axis_size("blk")
    my_index = lax.axis_index("blk")
    all_rows = embeds.shape[1]
    own_rows = all_rows // blocks
    heads_kv = prompt_key_slots.shape[1]
    slots_here = prompt_key_slots.shape[0]
    keys_here = slots_here * BLOCK_POSITIONS
    group_queries = QUERY_HEADS // KEY_VALUE_HEADS
    col_width = group_queries + 2
    score_scale = 1.0 / math.sqrt(HEAD_WIDTH)
    unit_count = w_gate.shape[1]
    beam_req = jnp.arange(all_rows, dtype=jnp.int32) // REQUEST_BEAMS
    tenant_beam = jnp.sum(
        (beam_req[:, None] >= tenant_bounds[None, 1:TENANT_COUNT]).astype(jnp.int32), axis=1
    )
    length_beam = jnp.repeat(prompt_length, REQUEST_BEAMS)
    slot_tenant = jnp.repeat(slot_table // PROMPT_BLOCKS, BLOCK_POSITIONS)
    slot_pos = jnp.repeat(slot_table % PROMPT_BLOCKS * BLOCK_POSITIONS, BLOCK_POSITIONS) + jnp.tile(
        jnp.arange(BLOCK_POSITIONS, dtype=jnp.int32), slots_here
    )
    visible = (tenant_beam[:, None] == slot_tenant[None, :]) & (
        slot_pos[None, :] < length_beam[:, None]
    )
    prompt_mask = visible[None, :, None, :]
    keys_flat = prompt_key_slots.transpose(1, 0, 2, 3).reshape(heads_kv, keys_here, HEAD_WIDTH)
    values_flat = prompt_value_slots.transpose(1, 0, 2, 3).reshape(heads_kv, keys_here, HEAD_WIDTH)
    local_beam = jnp.arange(own_rows, dtype=jnp.int32)
    base_rows = local_beam // REQUEST_BEAMS * REQUEST_BEAMS
    trailing_zeros = jnp.zeros((own_rows, heads_kv, DECODE_STEPS, HEAD_WIDTH), jnp.bfloat16)
    cached_key_rows = jnp.concatenate([generated_keys, trailing_zeros], axis=2)
    cached_value_rows = jnp.concatenate([generated_values, trailing_zeros], axis=2)
    gen_pos = jnp.arange(EARLIER_TOKENS + DECODE_STEPS, dtype=jnp.int32)
    w_both = jnp.concatenate([w_gate, w_up], axis=1)
    residual = embeds[0].astype(jnp.float32)
    squares = jnp.sum(residual * residual, axis=1)
    normed = (residual * attn_norm).astype(jnp.bfloat16)
    partial_value = jnp.dot(normed, query_key_value_weight, preferred_element_type=jnp.float32)
    own_value = scatter_sum(jnp.concatenate([partial_value, squares[:, None]], axis=1), "blk")
    inverse = lax.rsqrt(own_value[:, -1] / MODEL_WIDTH + 1e-05)
    own_proj = (own_value[:, :-1] * inverse[:, None]).reshape(
        own_rows, heads_kv, col_width, HEAD_WIDTH
    )
    own_length = lax.dynamic_slice_in_dim(length_beam, my_index * own_rows, own_rows, 0)
    own_angle = angles_for(own_length + EARLIER_TOKENS + 0, HEAD_WIDTH)
    own_queries = rotate(own_proj[:, :, :group_queries], own_angle[:, None, None, :]).astype(
        jnp.bfloat16
    )
    query_rows = lax.all_gather(own_queries, "blk", axis=0, tiled=True)
    new_key = rotate(own_proj[:, :, group_queries], own_angle[:, None, :]).astype(jnp.bfloat16)
    new_value = own_proj[:, :, group_queries + 1].astype(jnp.bfloat16)
    parent_rows = base_rows + parents[0]
    cached_key_rows = (
        jnp.take(cached_key_rows, parent_rows, axis=0).at[:, :, EARLIER_TOKENS].set(new_key)
    )
    cached_value_rows = (
        jnp.take(cached_value_rows, parent_rows, axis=0).at[:, :, EARLIER_TOKENS].set(new_value)
    )
    grouped = query_rows.transpose(1, 0, 2, 3).reshape(
        heads_kv, all_rows * group_queries, HEAD_WIDTH
    )
    scores = jnp.einsum("kqd,knd->kqn", grouped, keys_flat, preferred_element_type=jnp.float32)
    scores = scores.reshape(heads_kv, all_rows, group_queries, keys_here) * score_scale
    top_score = jnp.max(jnp.where(prompt_mask, scores, masked_score), axis=3)
    weights = jnp.where(prompt_mask, jnp.exp(scores - top_score[..., None]), 0.0)
    total_mass = jnp.sum(weights, axis=3)
    flat_weights = weights.reshape(heads_kv, all_rows * group_queries, keys_here).astype(
        jnp.bfloat16
    )
    summed = jnp.einsum(
        "kqn,knd->kqd", flat_weights, values_flat, preferred_element_type=jnp.float32
    )
    summed = summed.reshape(heads_kv, all_rows, group_queries, HEAD_WIDTH)
    packed = jnp.concatenate([summed, top_score[..., None], total_mass[..., None]], axis=3)
    packed = packed.transpose(1, 0, 2, 3).reshape(
        blocks, own_rows, heads_kv, group_queries, HEAD_WIDTH + 2
    )
    parts = lax.all_to_all(packed, "blk", 0, 0, tiled=False)
    part_top = parts[..., HEAD_WIDTH]
    prompt_top = jnp.max(part_top, axis=0)
    part_factor = jnp.exp(part_top - prompt_top[None])
    prompt_mass = jnp.sum(parts[..., HEAD_WIDTH + 1] * part_factor, axis=0)
    prompt_sum = jnp.sum(parts[..., :HEAD_WIDTH] * part_factor[..., None], axis=0)
    prompt_top = prompt_top.transpose(1, 0, 2)
    prompt_mass = prompt_mass.transpose(1, 0, 2)
    prompt_sum = prompt_sum.transpose(1, 0, 2, 3)
    gen_scores = (
        jnp.einsum(
            "bkgd,bknd->kbgn", own_queries, cached_key_rows, preferred_element_type=jnp.float32
        )
        * score_scale
    )
    live = (gen_pos <= EARLIER_TOKENS)[None, None, None, :]
    gen_top = jnp.max(jnp.where(live, gen_scores, masked_score), axis=3)
    best = jnp.maximum(prompt_top, gen_top)
    gen_weights = jnp.where(live, jnp.exp(gen_scores - best[..., None]), 0.0)
    shift = jnp.exp(prompt_top - best)
    full_mass = prompt_mass * shift + jnp.sum(gen_weights, axis=3)
    gen_sum = jnp.einsum(
        "kbgn,bknd->kbgd",
        gen_weights.astype(jnp.bfloat16),
        cached_value_rows,
        preferred_element_type=jnp.float32,
    )
    attended_output = (prompt_sum * shift[..., None] + gen_sum) / full_mass[..., None]
    heads_out = (
        attended_output.transpose(1, 0, 2, 3)
        .reshape(own_rows, heads_kv * group_queries * HEAD_WIDTH)
        .astype(jnp.bfloat16)
    )
    head_part = jnp.dot(
        lax.all_gather(heads_out, "blk", axis=0, tiled=True),
        w_out,
        preferred_element_type=jnp.float32,
    )
    after_attn = residual + across_heads(head_part)
    squares2 = jnp.sum(after_attn * after_attn, axis=1)
    normed2 = (after_attn * mlp_norm).astype(jnp.bfloat16)
    mixed = scatter_sum(
        jnp.concatenate(
            [jnp.dot(normed2, w_both, preferred_element_type=jnp.float32), squares2[:, None]],
            axis=1,
        ),
        "blk",
    )
    own_inverse = lax.rsqrt(mixed[:, -1] / MODEL_WIDTH + 1e-05)
    gate = mixed[:, :unit_count] * own_inverse[:, None]
    upper = mixed[:, unit_count : 2 * unit_count] * own_inverse[:, None]
    hidden = (jax.nn.silu(gate) * upper).astype(jnp.bfloat16)
    ff_part = jnp.dot(
        lax.all_gather(hidden, "blk", axis=0, tiled=True),
        w_down,
        preferred_element_type=jnp.float32,
    )
    outputs = [after_attn + across_heads(ff_part)]
    return (jnp.stack(outputs), cached_key_rows, cached_value_rows)


def solution(mesh):
    in_specs = (
        P(None, None, "blk"),
        P("blk"),
        P("blk", "kv"),
        P("kv", "blk"),
        P("blk"),
        P("blk", "kv"),
        P("blk", "kv"),
        P("kv", "blk"),
        P("blk", "kv", None, None),
        P("blk", "kv", None, None),
        P("blk", "kv", None, None),
        P("blk", "kv", None, None),
        P(None, "blk"),
        P(),
        P(),
        P("blk"),
    )
    out_specs = (P(None, None, "blk"), P("blk", "kv", None, None), P("blk", "kv", None, None))
    return jax.shard_map(body, mesh=mesh, in_specs=in_specs, out_specs=out_specs, check_vma=False)
```

profile of v0, /device:TPU:2, one launch (start us, length us, event | category | flops | bytes accessed | tf_op | source)
XLA Modules:
  0.0 210.3 jit_solution(3467085731439705462)
XLA Ops:
  0.7 1.0 copy.159
  1.7 0.8 fusion.23
  2.7 1.1 fusion.21
  3.9 0.9 pad_maximum_fusion.1
  4.8 7.6 %all-to-all-start = ((f32[32,8,641]{2,1,0:T(8,128)}), f32[32,8,641]{2,1,0:T(8,128)S(1)}, u32[]{:S(2)}, u32[]{:S(2)}) async-start(f32[32,8,641]{2,1,0:T(8,128)} %pad_maximum_fusion.1), calls=%async_computation | async-start | bytes 1572864 | tf_op jit(solution)/shard_map/all_to_all | solution.py:37
  14.6 1.0 compare_and_fusion
  15.5 0.9 bitcast_select_fusion.1
  16.4 9.3 %all-to-all-done = f32[32,8,641]{2,1,0:T(8,128)S(1)} async-done(((f32[32,8,641]{2,1,0:T(8,128)}), f32[32,8,641]{2,1,0:T(8,128)S(1)}, u32[]{:S(2)}, u32[]{:S(2)}) %all-to-all-start) | async-done | bytes 656416 | tf_op jit(solution)/shard_map/all_to_all | solution.py:37
  26.2 22.9 %all_gather.9 = bf16[256,1,3,128]{3,0,2,1:T(8,128)(2,1)S(1)} all-gather(bf16[8,1,3,128]{3,0,2,1:T(8,128)(2,1)S(1)} %pad_maximum_fusion.2), channel_id=1, replica_groups=mesh['kv'=8,'blk'=32] {'blk'}, dimensions={0}, use_global_device_ids=true | all-gather | bytes 202752 | tf_op jit(solution)/shard_map/all_gather | solution.py:126
  49.0 1.8 select_reduce_fusion
  50.9 3.1 %fusion.2 = (bf16[32,8,3,1024]{3,1,0,2:T(8,128)(2,1)}, f32[256,3]{0,1:T(4,128)S(1)}) fusion(f32[256,3,1024]{2,0,1:T(8,128)S(1)} %get-tuple-element.71, f32[256,3]{0,1:T(4,128)S(1)} %get-tuple-element.70, pred[256,1024]{1,0:T(8,128)(4,1)} %compare_and_fusion), kind=kLoop, calls=%fused_computation.8 | loop fusion | flops 3931392 | bytes 4986880 | tf_op jit(solution)/shard_map/reshape.462
  54.1 0.6 copy.163
  54.7 0.6 copy.162
  55.4 2.0 fusion.5
  57.4 1.1 maximum_bitcast_fusion
  58.5 5.7 %all-to-all-start.1 = ((f32[32,8,1,3,130]{4,1,3,2,0:T(8,128)}), f32[32,8,1,3,130]{4,1,3,2,0:T(8,128)S(1)}, u32[]{:S(2)}, u32[]{:S(2)}) async-start(f32[32,8,1,3,130]{4,1,3,2,0:T(8,128)} %maximum_bitcast_fusion), calls=%async_computation.1 | async-start | bytes 1572864 | tf_op jit(solution)/shard_map/all_to_all | solution.py:155
  65.1 12.5 %all-to-all-done.1 = f32[32,8,1,3,130]{4,1,3,2,0:T(8,128)S(1)} async-done(((f32[32,8,1,3,130]{4,1,3,2,0:T(8,128)}), f32[32,8,1,3,130]{4,1,3,2,0:T(8,128)S(1)}, u32[]{:S(2)}, u32[]{:S(2)}) %all-to-all-start.1) | async-done | bytes 399392 | tf_op jit(solution)/shard_map/all_to_all | solution.py:155
  79.5 23.1 %all_gather.10 = bf16[256,384]{1,0:T(8,128)(2,1)S(1)} all-gather(bf16[8,384]{1,0:T(8,128)(2,1)S(1)} %bitcast.108), channel_id=1, replica_groups=mesh['kv'=8,'blk'=32] {'blk'}, dimensions={0}, use_global_device_ids=true | all-gather | bytes 202752 | tf_op jit(solution)/shard_map/all_gather | solution.py:189
  102.8 2.0 collective-permute-start
  104.8 3.3 %collective-permute-done = f32[256,96]{0,1:T(8,128)S(1)} collective-permute-done((f32[256,96]{0,1:T(8,128)S(1)}, f32[256,96]{0,1:T(8,128)S(1)}, u32[]{:S(2)}, u32[]{:S(2)}) %collective-permute-start) | collective-permute-done | bytes 98336 | tf_op jit(solution)/shard_map/ppermute | solution.py:22
  108.1 3.4 %collective-permute-start.1 = (f32[256,96]{0,1:T(8,128)S(1)}, f32[256,96]{0,1:T(8,128)S(1)}, u32[]{:S(2)}, u32[]{:S(2)}) collective-permute-start(f32[256,96]{0,1:T(8,128)S(1)} %add.109), channel_id=1, source_target_pairs={{0,64},{32,96},{64,0},{96,32},{128,192},{160,224},{192,128},{224,1... | collective-permute-start | bytes 294920 | tf_op jit(solution)/shard_map/ppermute | solution.py:22
  111.4 4.8 %collective-permute-done.1 = f32[256,96]{0,1:T(8,128)S(1)} collective-permute-done((f32[256,96]{0,1:T(8,128)S(1)}, f32[256,96]{0,1:T(8,128)S(1)}, u32[]{:S(2)}, u32[]{:S(2)}) %collective-permute-start.1) | collective-permute-done | bytes 98336 | tf_op jit(solution)/shard_map/ppermute | solution.py:22
  116.3 6.3 %collective-permute-start.2 = (f32[256,96]{0,1:T(8,128)S(1)}, f32[256,96]{0,1:T(8,128)S(1)}, u32[]{:S(2)}, u32[]{:S(2)}) collective-permute-start(f32[256,96]{0,1:T(8,128)S(1)} %add.110), channel_id=1, source_target_pairs={{0,128},{32,160},{64,192},{96,224},{128,0},{160,32},{192,64},{224,... | collective-permute-start | bytes 294920 | tf_op jit(solution)/shard_map/ppermute | solution.py:22
  122.5 3.6 %collective-permute-done.2 = f32[256,96]{0,1:T(8,128)S(1)} collective-permute-done((f32[256,96]{0,1:T(8,128)S(1)}, f32[256,96]{0,1:T(8,128)S(1)}, u32[]{:S(2)}, u32[]{:S(2)}) %collective-permute-start.2) | collective-permute-done | bytes 98336 | tf_op jit(solution)/shard_map/ppermute | solution.py:22
  127.2 34.6 %all_to_all.15 = f32[32,8,2049]{2,1,0:T(8,128)S(1)} all-to-all(f32[32,8,2049]{2,1,0:T(8,128)S(1)} %pad_maximum_fusion), channel_id=1, replica_groups=mesh['kv'=8,'blk'=32] {'blk'}, dimensions={0} | all-to-all | bytes 4196352 | tf_op jit(solution)/shard_map/all_to_all | solution.py:37
  162.1 23.3 %all_gather.11 = bf16[256,1024]{1,0:T(8,128)(2,1)S(1)} all-gather(bf16[8,1024]{1,0:T(8,128)(2,1)S(1)} %fusion.28), channel_id=1, replica_groups=mesh['kv'=8,'blk'=32] {'blk'}, dimensions={0}, use_global_device_ids=true | all-gather | bytes 540672 | tf_op jit(solution)/shard_map/all_gather | solution.py:208
  185.9 5.0 %collective-permute-done.3 = f32[256,96]{0,1:T(8,128)S(1)} collective-permute-done((f32[256,96]{0,1:T(8,128)S(1)}, f32[256,96]{0,1:T(8,128)S(1)}, u32[]{:S(2)}, u32[]{:S(2)}) %collective-permute-start.3) | collective-permute-done | bytes 98336 | tf_op jit(solution)/shard_map/ppermute | solution.py:22
  190.9 3.3 %collective-permute-start.4 = (f32[256,96]{0,1:T(8,128)S(1)}, f32[256,96]{0,1:T(8,128)S(1)}, u32[]{:S(2)}, u32[]{:S(2)}) collective-permute-start(f32[256,96]{0,1:T(8,128)S(1)} %add.115), channel_id=1, source_target_pairs={{0,64},{32,96},{64,0},{96,32},{128,192},{160,224},{192,128},{224,1... | collective-permute-start | bytes 294920 | tf_op jit(solution)/shard_map/ppermute | solution.py:22
  194.2 4.8 %collective-permute-done.4 = f32[256,96]{0,1:T(8,128)S(1)} collective-permute-done((f32[256,96]{0,1:T(8,128)S(1)}, f32[256,96]{0,1:T(8,128)S(1)}, u32[]{:S(2)}, u32[]{:S(2)}) %collective-permute-start.4) | collective-permute-done | bytes 98336 | tf_op jit(solution)/shard_map/ppermute | solution.py:22
  199.0 4.3 %collective-permute-start.5 = (f32[256,96]{0,1:T(8,128)S(1)}, f32[256,96]{0,1:T(8,128)S(1)}, u32[]{:S(2)}, u32[]{:S(2)}) collective-permute-start(f32[256,96]{0,1:T(8,128)S(1)} %add.116), channel_id=1, source_target_pairs={{0,128},{32,160},{64,192},{96,224},{128,0},{160,32},{192,64},{224,... | collective-permute-start | bytes 294920 | tf_op jit(solution)/shard_map/ppermute | solution.py:22
  203.4 6.2 %collective-permute-done.5 = f32[256,96]{0,1:T(8,128)S(1)} collective-permute-done((f32[256,96]{0,1:T(8,128)S(1)}, f32[256,96]{0,1:T(8,128)S(1)}, u32[]{:S(2)}, u32[]{:S(2)}) %collective-permute-start.5) | collective-permute-done | bytes 98336 | tf_op jit(solution)/shard_map/ppermute | solution.py:22
  209.6 0.7 add_bitcast_fusion
  (103 shorter events, 7.5 us)
Async XLA Ops:
  0.6 48.4 %copy-start = (bf16[8,1,128,128]{3,2,1,0:T(8,128)(2,1)S(1)}, bf16[8,1,128,128]{3,2,1,0:T(8,128)(2,1)}, u32[]{:S(2)}) copy-start(bf16[8,1,128,128]{3,2,1,0:T(8,128)(2,1)} %param.30) | copy-start | bytes 786436
  0.6 11.8 %copy-start.12 = (s32[32]{0:T(128)S(1)}, s32[32]{0:T(128)}, u32[]{:S(2)}) copy-start(s32[32]{0:T(128)} %param.35) | copy-start | bytes 388
  0.7 12.0 %copy-start.14 = (s32[8]{0:T(128)S(1)}, s32[8]{0:T(128)}, u32[]{:S(2)}) copy-start(s32[8]{0:T(128)} %param.37) | copy-start | bytes 100
  0.7 12.0 %copy-start.15 = (s32[1,8]{1,0:T(1,128)S(1)}, s32[1,8]{1,0:T(1,128)}, u32[]{:S(2)}) copy-start(s32[1,8]{1,0:T(1,128)} %param.34) | copy-start | bytes 100
  0.7 12.1 %copy-start.6 = (bf16[8,1,127,128]{3,0,2,1:T(8,128)(2,1)S(1)}, bf16[8,1,127,128]{3,0,2,1:T(8,128)(2,1)}, u32[]{:S(2)}) copy-start(bf16[8,1,127,128]{3,0,2,1:T(8,128)(2,1)} %param.32) | copy-start | bytes 780292
  0.7 12.1 %copy-start.7 = (bf16[8,1,127,128]{3,0,2,1:T(8,128)(2,1)S(1)}, bf16[8,1,127,128]{3,0,2,1:T(8,128)(2,1)}, u32[]{:S(2)}) copy-start(bf16[8,1,127,128]{3,0,2,1:T(8,128)(2,1)} %param.33) | copy-start | bytes 780292
  2.7 10.5 %copy-start.16 = (s32[5]{0:T(128)S(1)}, s32[5]{0:T(128)}, u32[]{:S(2)}) copy-start(s32[5]{0:T(128)} %param.36) | copy-start | bytes 64
  4.8 20.9 %all-to-all-start = ((f32[32,8,641]{2,1,0:T(8,128)}), f32[32,8,641]{2,1,0:T(8,128)S(1)}, u32[]{:S(2)}, u32[]{:S(2)}) async-start(f32[32,8,641]{2,1,0:T(8,128)} %pad_maximum_fusion.1), calls=%async_computation | async-start | bytes 1572864 | tf_op jit(solution)/shard_map/all_to_all | solution.py:37
  54.7 9.7 %copy-start.1 = (bf16[8,1,128,128]{3,2,0,1:T(8,128)(2,1)S(1)}, bf16[8,1,128,128]{3,2,0,1:T(8,128)(2,1)}, u32[]{:S(2)}) copy-start(bf16[8,1,128,128]{3,2,0,1:T(8,128)(2,1)} %get-tuple-element.66) | copy-start | bytes 786436
  55.4 9.6 %copy-start.4 = (bf16[8,1,128,128]{3,2,0,1:T(8,128)(2,1)S(1)}, bf16[8,1,128,128]{3,2,0,1:T(8,128)(2,1)}, u32[]{:S(2)}) copy-start(bf16[8,1,128,128]{3,2,0,1:T(8,128)(2,1)} %get-tuple-element.67) | copy-start | bytes 786436
  58.5 44.1 %copy-start.11 = (bf16[384,96]{0,1:T(8,128)(2,1)S(1)}, bf16[384,96]{0,1:T(8,128)(2,1)}, u32[]{:S(2)}) copy-start(bf16[384,96]{0,1:T(8,128)(2,1)} %param.25) | copy-start | bytes 221188
  58.5 67.7 %copy-start.3 = (bf16[1,256,96]{1,2,0:T(8,128)(2,1)S(1)}, bf16[1,256,96]{1,2,0:T(8,128)(2,1)}, u32[]{:S(2)}) copy-start(bf16[1,256,96]{1,2,0:T(8,128)(2,1)} %param.22) | copy-start | bytes 147460
  58.5 68.0 %copy-start.8 = (bf16[96,1024]{1,0:T(8,128)(2,1)S(1)}, bf16[96,1024]{1,0:T(8,128)(2,1)}, u32[]{:S(2)}) copy-start(bf16[96,1024]{1,0:T(8,128)(2,1)} %param.28) | copy-start | bytes 589828
  58.5 68.0 %copy-start.9 = (bf16[96,1024]{1,0:T(8,128)(2,1)S(1)}, bf16[96,1024]{1,0:T(8,128)(2,1)}, u32[]{:S(2)}) copy-start(bf16[96,1024]{1,0:T(8,128)(2,1)} %param.27) | copy-start | bytes 589828
  58.5 68.0 %copy-start.13 = (f32[96]{0:T(128)S(1)}, f32[96]{0:T(128)}, u32[]{:S(2)}) copy-start(f32[96]{0:T(128)} %param.26) | copy-start | bytes 1156
  58.5 19.0 %all-to-all-start.1 = ((f32[32,8,1,3,130]{4,1,3,2,0:T(8,128)}), f32[32,8,1,3,130]{4,1,3,2,0:T(8,128)S(1)}, u32[]{:S(2)}, u32[]{:S(2)}) async-start(f32[32,8,1,3,130]{4,1,3,2,0:T(8,128)} %maximum_bitcast_fusion), calls=%async_computation.1 | async-start | bytes 1572864 | tf_op jit(solution)/shard_map/all_to_all | solution.py:155
  64.5 62.5 %copy-start.2 = (bf16[8,1,128,128]{3,2,0,1:T(8,128)(2,1)}, bf16[8,1,128,128]{3,2,0,1:T(8,128)(2,1)S(1)}, u32[]{:S(2)}) copy-start(bf16[8,1,128,128]{3,2,0,1:T(8,128)(2,1)S(1)} %scatter.6) | copy-start | bytes 786436
  65.0 62.0 %copy-start.5 = (bf16[8,1,128,128]{3,2,0,1:T(8,128)(2,1)}, bf16[8,1,128,128]{3,2,0,1:T(8,128)(2,1)S(1)}, u32[]{:S(2)}) copy-start(bf16[8,1,128,128]{3,2,0,1:T(8,128)(2,1)S(1)} %scatter.9) | copy-start | bytes 786436
  102.8 5.3 %collective-permute-start = (f32[256,96]{0,1:T(8,128)S(1)}, f32[256,96]{0,1:T(8,128)S(1)}, u32[]{:S(2)}, u32[]{:S(2)}) collective-permute-start(f32[256,96]{0,1:T(8,128)S(1)} %fusion.62), channel_id=1, source_target_pairs={{0,32},{32,0},{64,96},{96,64},{128,160},{160,128},{192,224},{224,1... | collective-permute-start | bytes 294920 | tf_op jit(solution)/shard_map/ppermute | solution.py:22
  108.1 8.2 %collective-permute-start.1 = (f32[256,96]{0,1:T(8,128)S(1)}, f32[256,96]{0,1:T(8,128)S(1)}, u32[]{:S(2)}, u32[]{:S(2)}) collective-permute-start(f32[256,96]{0,1:T(8,128)S(1)} %add.109), channel_id=1, source_target_pairs={{0,64},{32,96},{64,0},{96,32},{128,192},{160,224},{192,128},{224,1... | collective-permute-start | bytes 294920 | tf_op jit(solution)/shard_map/ppermute | solution.py:22
  116.3 9.9 %collective-permute-start.2 = (f32[256,96]{0,1:T(8,128)S(1)}, f32[256,96]{0,1:T(8,128)S(1)}, u32[]{:S(2)}, u32[]{:S(2)}) collective-permute-start(f32[256,96]{0,1:T(8,128)S(1)} %add.110), channel_id=1, source_target_pairs={{0,128},{32,160},{64,192},{96,224},{128,0},{160,32},{192,64},{224,... | collective-permute-start | bytes 294920 | tf_op jit(solution)/shard_map/ppermute | solution.py:22
  127.2 58.3 %copy-start.10 = (bf16[1024,96]{0,1:T(8,128)(2,1)S(1)}, bf16[1024,96]{0,1:T(8,128)(2,1)}, u32[]{:S(2)}) copy-start(bf16[1024,96]{0,1:T(8,128)(2,1)} %param.29) | copy-start | bytes 589828
  185.8 5.1 %collective-permute-start.3 = (f32[256,96]{0,1:T(8,128)S(1)}, f32[256,96]{0,1:T(8,128)S(1)}, u32[]{:S(2)}, u32[]{:S(2)}) collective-permute-start(f32[256,96]{0,1:T(8,128)S(1)} %fusion.63), channel_id=1, source_target_pairs={{0,32},{32,0},{64,96},{96,64},{128,160},{160,128},{192,224},{224,1... | collective-permute-start | bytes 294920 | tf_op jit(solution)/shard_map/ppermute | solution.py:22
  190.9 8.1 %collective-permute-start.4 = (f32[256,96]{0,1:T(8,128)S(1)}, f32[256,96]{0,1:T(8,128)S(1)}, u32[]{:S(2)}, u32[]{:S(2)}) collective-permute-start(f32[256,96]{0,1:T(8,128)S(1)} %add.115), channel_id=1, source_target_pairs={{0,64},{32,96},{64,0},{96,32},{128,192},{160,224},{192,128},{224,1... | collective-permute-start | bytes 294920 | tf_op jit(solution)/shard_map/ppermute | solution.py:22
  199.0 10.6 %collective-permute-start.5 = (f32[256,96]{0,1:T(8,128)S(1)}, f32[256,96]{0,1:T(8,128)S(1)}, u32[]{:S(2)}, u32[]{:S(2)}) collective-permute-start(f32[256,96]{0,1:T(8,128)S(1)} %add.116), channel_id=1, source_target_pairs={{0,128},{32,160},{64,192},{96,224},{128,0},{160,32},{192,64},{224,... | collective-permute-start | bytes 294920 | tf_op jit(solution)/shard_map/ppermute | solution.py:22
where the time goes:
time: 211 us; the launch traced here: 210 us
  blocking collectives  104 us (49%)
  waiting for transfers between devices  49.7 us (24%)
  starting transfers between devices  32.7 us (15%)
  other arithmetic  10.9 us (5%)
  matrix products  6.5 us (3%)
  local copies, waits for them, and re-layouts  5.57 us (3%)
    all_to_all x1, blocking collectives, scatter_sum(): return jnp.sum(lax.all_to_all(pieces, axis, 0, 0, tiled=False), axis=0)  34.6 us
    ppermute x6, waiting for transfers between devices, exchange(): return lax.ppermute(value, axis, [(i, i ^ 1 << bit) for i in range(count)])  27.9 us
    all_gather x1, blocking collectives, body(): lax.all_gather(hidden, 'blk', axis=0, tiled=True)  23.3 us
    all_gather x1, blocking collectives, body(): lax.all_gather(heads_out, 'blk', axis=0, tiled=True)  23.1 us
    all_gather x1, blocking collectives, body(): query_rows = lax.all_gather(own_queries, 'blk', axis=0, tiled=True)  22.9 us
    ppermute x6, starting transfers between devices, exchange(): return lax.ppermute(value, axis, [(i, i ^ 1 << bit) for i in range(count)])  19.3 us
    all_to_all x1, waiting for transfers between devices, body(): parts = lax.all_to_all(packed, 'blk', 0, 0, tiled=False)  12.5 us
    all_to_all x1, waiting for transfers between devices, scatter_sum(): return jnp.sum(lax.all_to_all(pieces, axis, 0, 0, tiled=False), axis=0)  9.32 us
  transfers between devices with their start and end apart: 8, of which 8 were waited for; matrix products, arithmetic and copies ran while one was open for 2% of the time, Pallas kernels for 0%

commit v1 on v0

--- a/solution.py
+++ b/solution.py
@@ -1,3 +1,4 @@
+import functools
 import math
 import jax
 import jax.numpy as jnp
@@ -15,6 +16,19 @@
 EARLIER_TOKENS = 127
 DECODE_STEPS = 1
 masked_score = -1e30
+
+
+def _feed_sections(inp, lane_axis, dim_k):
+    return jax.lax.all_to_all(
+        jnp.concatenate([inp] * jax.lax.psum(1, lane_axis), axis=dim_k),
+        lane_axis,
+        dim_k,
+        dim_k,
+        tiled=True,
+    )
+
+
+advance_arrays = functools.partial(_feed_sections, lane_axis="blk", dim_k=0)
 
 
 def exchange(value, axis, bit):
@@ -204,11 +218,7 @@
     gate = mixed[:, :unit_count] * own_inverse[:, None]
     upper = mixed[:, unit_count : 2 * unit_count] * own_inverse[:, None]
     hidden = (jax.nn.silu(gate) * upper).astype(jnp.bfloat16)
-    ff_part = jnp.dot(
-        lax.all_gather(hidden, "blk", axis=0, tiled=True),
-        w_down,
-        preferred_element_type=jnp.float32,
-    )
+    ff_part = jnp.dot(advance_arrays(hidden), w_down, preferred_element_type=jnp.float32)
     outputs = [after_attn + across_heads(ff_part)]
     return (jnp.stack(outputs), cached_key_rows, cached_value_rows)
 

time: 211 us -> 203 us (0.962)
  blocking collectives: 104 us -> 95.6 us
    all_gather x1 -> x0, blocking collectives: 23.3 us -> none  [body(): lax.all_gather(hidden, 'blk', axis=0, tiled=True)]
    all_to_all x0 -> x1, blocking collectives: none -> 15.1 us  [_feed_sections(): jax.lax.all_to_all(jnp.concatenate([inp] * jax.lax.psum(1, lane_axis), ax...]
where the time goes in v1:
time: 203 us; the launch traced here: 202 us
  blocking collectives  95.6 us (47%)
  waiting for transfers between devices  49.7 us (24%)
  starting transfers between devices  32.7 us (16%)
  other arithmetic  10.9 us (5%)
  matrix products  6.5 us (3%)
  local copies, waits for them, and re-layouts  5.68 us (3%)
    all_to_all x1, blocking collectives, scatter_sum(): return jnp.sum(lax.all_to_all(pieces, axis, 0, 0, tiled=False), axis=0)  34.5 us
    ppermute x6, waiting for transfers between devices, exchange(): return lax.ppermute(value, axis, [(i, i ^ 1 << bit) for i in range(count)])  27.9 us
    all_gather x1, blocking collectives, body(): lax.all_gather(heads_out, 'blk', axis=0, tiled=True)  23.1 us
    all_gather x1, blocking collectives, body(): query_rows = lax.all_gather(own_queries, 'blk', axis=0, tiled=True)  22.9 us
    ppermute x6, starting transfers between devices, exchange(): return lax.ppermute(value, axis, [(i, i ^ 1 << bit) for i in range(count)])  19.3 us
    all_to_all x1, blocking collectives, _feed_sections(): jax.lax.all_to_all(jnp.concatenate([inp] * jax.lax.psum(1, lane_axis), ax...  15.1 us
    all_to_all x1, waiting for transfers between devices, body(): parts = lax.all_to_all(packed, 'blk', 0, 0, tiled=False)  12.5 us
    all_to_all x1, waiting for transfers between devices, scatter_sum(): return jnp.sum(lax.all_to_all(pieces, axis, 0, 0, tiled=False), axis=0)  9.32 us
  transfers between devices with their start and end apart: 8, of which 8 were waited for; matrix products, arithmetic and copies ran while one was open for 2% of the time, Pallas kernels for 0%

profile of v1, /device:TPU:2, one launch (start us, length us, event | category | flops | bytes accessed | tf_op | source)
XLA Modules:
  0.0 202.4 jit_solution(18270273555033511758)
XLA Ops:
  0.7 1.0 copy.159
  1.7 0.8 fusion.25
  2.7 1.1 fusion.23
  3.9 0.9 pad_maximum_fusion.1
  4.8 7.6 %all-to-all-start = ((f32[32,8,641]{2,1,0:T(8,128)}), f32[32,8,641]{2,1,0:T(8,128)S(1)}, u32[]{:S(2)}, u32[]{:S(2)}) async-start(f32[32,8,641]{2,1,0:T(8,128)} %pad_maximum_fusion.1), calls=%async_computation | async-start | bytes 1572864 | tf_op jit(solution)/shard_map/all_to_all | solution.py:51
  14.6 1.0 compare_and_fusion
  15.5 0.9 bitcast_select_fusion.1
  16.4 9.3 %all-to-all-done = f32[32,8,641]{2,1,0:T(8,128)S(1)} async-done(((f32[32,8,641]{2,1,0:T(8,128)}), f32[32,8,641]{2,1,0:T(8,128)S(1)}, u32[]{:S(2)}, u32[]{:S(2)}) %all-to-all-start) | async-done | bytes 656416 | tf_op jit(solution)/shard_map/all_to_all | solution.py:51
  26.2 22.9 %all_gather.6 = bf16[256,1,3,128]{3,0,2,1:T(8,128)(2,1)S(1)} all-gather(bf16[8,1,3,128]{3,0,2,1:T(8,128)(2,1)S(1)} %pad_maximum_fusion.2), channel_id=1, replica_groups=mesh['kv'=8,'blk'=32] {'blk'}, dimensions={0}, use_global_device_ids=true | all-gather | bytes 202752 | tf_op jit(solution)/shard_map/all_gather | solution.py:140
  49.0 1.8 select_reduce_fusion
  50.9 3.1 %fusion.2 = (bf16[32,8,3,1024]{3,1,0,2:T(8,128)(2,1)}, f32[256,3]{0,1:T(4,128)S(1)}) fusion(f32[256,3,1024]{2,0,1:T(8,128)S(1)} %get-tuple-element.73, f32[256,3]{0,1:T(4,128)S(1)} %get-tuple-element.72, pred[256,1024]{1,0:T(8,128)(4,1)} %compare_and_fusion), kind=kLoop, calls=%fused_computation.8 | loop fusion | flops 3931392 | bytes 4986880 | tf_op jit(solution)/shard_map/reshape.464
  54.1 0.6 copy.163
  54.7 0.6 copy.162
  55.4 2.0 %fusion.5 = f32[32,8,1,3,128]{4,1,3,0,2:T(8,128)S(1)} fusion(bf16[1024,128,1,1]{1,0,3,2:T(8,128)(2,1)} %bitcast.113, bf16[32,8,3,1024]{3,1,0,2:T(8,128)(2,1)} %get-tuple-element.57), kind=kOutput, calls=%fused_computation.11 | convolution fusion | flops 201326592 | bytes 2228224 | tf_op jit(solution)/shard_map/kqn,knd->kqd/dot_general | solution.py:161
  57.4 1.1 maximum_bitcast_fusion
  58.5 5.7 %all-to-all-start.1 = ((f32[32,8,1,3,130]{4,1,3,2,0:T(8,128)}), f32[32,8,1,3,130]{4,1,3,2,0:T(8,128)S(1)}, u32[]{:S(2)}, u32[]{:S(2)}) async-start(f32[32,8,1,3,130]{4,1,3,2,0:T(8,128)} %maximum_bitcast_fusion), calls=%async_computation.1 | async-start | bytes 1572864 | tf_op jit(solution)/shard_map/all_to_all | solution.py:169
  65.0 12.5 %all-to-all-done.1 = f32[32,8,1,3,130]{4,1,3,2,0:T(8,128)S(1)} async-done(((f32[32,8,1,3,130]{4,1,3,2,0:T(8,128)}), f32[32,8,1,3,130]{4,1,3,2,0:T(8,128)S(1)}, u32[]{:S(2)}, u32[]{:S(2)}) %all-to-all-start.1) | async-done | bytes 399392 | tf_op jit(solution)/shard_map/all_to_all | solution.py:169
  79.5 23.1 %all_gather.7 = bf16[256,384]{1,0:T(8,128)(2,1)S(1)} all-gather(bf16[8,384]{1,0:T(8,128)(2,1)S(1)} %bitcast.112), channel_id=1, replica_groups=mesh['kv'=8,'blk'=32] {'blk'}, dimensions={0}, use_global_device_ids=true | all-gather | bytes 202752 | tf_op jit(solution)/shard_map/all_gather | solution.py:203
  102.8 2.0 collective-permute-start
  104.8 3.3 %collective-permute-done = f32[256,96]{0,1:T(8,128)S(1)} collective-permute-done((f32[256,96]{0,1:T(8,128)S(1)}, f32[256,96]{0,1:T(8,128)S(1)}, u32[]{:S(2)}, u32[]{:S(2)}) %collective-permute-start) | collective-permute-done | bytes 98336 | tf_op jit(solution)/shard_map/ppermute | solution.py:36
  108.1 3.3 %collective-permute-start.1 = (f32[256,96]{0,1:T(8,128)S(1)}, f32[256,96]{0,1:T(8,128)S(1)}, u32[]{:S(2)}, u32[]{:S(2)}) collective-permute-start(f32[256,96]{0,1:T(8,128)S(1)} %add.109), channel_id=1, source_target_pairs={{0,64},{32,96},{64,0},{96,32},{128,192},{160,224},{192,128},{224,1... | collective-permute-start | bytes 294920 | tf_op jit(solution)/shard_map/ppermute | solution.py:36
  111.4 4.8 %collective-permute-done.1 = f32[256,96]{0,1:T(8,128)S(1)} collective-permute-done((f32[256,96]{0,1:T(8,128)S(1)}, f32[256,96]{0,1:T(8,128)S(1)}, u32[]{:S(2)}, u32[]{:S(2)}) %collective-permute-start.1) | collective-permute-done | bytes 98336 | tf_op jit(solution)/shard_map/ppermute | solution.py:36
  116.3 6.3 %collective-permute-start.2 = (f32[256,96]{0,1:T(8,128)S(1)}, f32[256,96]{0,1:T(8,128)S(1)}, u32[]{:S(2)}, u32[]{:S(2)}) collective-permute-start(f32[256,96]{0,1:T(8,128)S(1)} %add.110), channel_id=1, source_target_pairs={{0,128},{32,160},{64,192},{96,224},{128,0},{160,32},{192,64},{224,... | collective-permute-start | bytes 294920 | tf_op jit(solution)/shard_map/ppermute | solution.py:36
  122.5 3.6 %collective-permute-done.2 = f32[256,96]{0,1:T(8,128)S(1)} collective-permute-done((f32[256,96]{0,1:T(8,128)S(1)}, f32[256,96]{0,1:T(8,128)S(1)}, u32[]{:S(2)}, u32[]{:S(2)}) %collective-permute-start.2) | collective-permute-done | bytes 98336 | tf_op jit(solution)/shard_map/ppermute | solution.py:36
  127.2 34.5 %all_to_all.27 = f32[32,8,2049]{2,1,0:T(8,128)S(1)} all-to-all(f32[32,8,2049]{2,1,0:T(8,128)S(1)} %pad_maximum_fusion), channel_id=1, replica_groups=mesh['kv'=8,'blk'=32] {'blk'}, dimensions={0} | all-to-all | bytes 4196352 | tf_op jit(solution)/shard_map/all_to_all | solution.py:51
  162.3 15.1 %all_to_all.28 = bf16[32,8,1024]{2,1,0:T(8,128)(2,1)S(1)} all-to-all(bf16[32,8,1024]{2,1,0:T(8,128)(2,1)S(1)} %bitcast.108), channel_id=1, replica_groups=mesh['kv'=8,'blk'=32] {'blk'}, dimensions={0} | all-to-all | bytes 1048576 | tf_op jit(solution)/shard_map/all_to_all | solution.py:22
  177.9 5.0 %collective-permute-done.3 = f32[256,96]{0,1:T(8,128)S(1)} collective-permute-done((f32[256,96]{0,1:T(8,128)S(1)}, f32[256,96]{0,1:T(8,128)S(1)}, u32[]{:S(2)}, u32[]{:S(2)}) %collective-permute-start.3) | collective-permute-done | bytes 98336 | tf_op jit(solution)/shard_map/ppermute | solution.py:36
  183.0 3.2 %collective-permute-start.4 = (f32[256,96]{0,1:T(8,128)S(1)}, f32[256,96]{0,1:T(8,128)S(1)}, u32[]{:S(2)}, u32[]{:S(2)}) collective-permute-start(f32[256,96]{0,1:T(8,128)S(1)} %add.115), channel_id=1, source_target_pairs={{0,64},{32,96},{64,0},{96,32},{128,192},{160,224},{192,128},{224,1... | collective-permute-start | bytes 294920 | tf_op jit(solution)/shard_map/ppermute | solution.py:36
  186.2 4.8 %collective-permute-done.4 = f32[256,96]{0,1:T(8,128)S(1)} collective-permute-done((f32[256,96]{0,1:T(8,128)S(1)}, f32[256,96]{0,1:T(8,128)S(1)}, u32[]{:S(2)}, u32[]{:S(2)}) %collective-permute-start.4) | collective-permute-done | bytes 98336 | tf_op jit(solution)/shard_map/ppermute | solution.py:36
  191.1 4.4 %collective-permute-start.5 = (f32[256,96]{0,1:T(8,128)S(1)}, f32[256,96]{0,1:T(8,128)S(1)}, u32[]{:S(2)}, u32[]{:S(2)}) collective-permute-start(f32[256,96]{0,1:T(8,128)S(1)} %add.116), channel_id=1, source_target_pairs={{0,128},{32,160},{64,192},{96,224},{128,0},{160,32},{192,64},{224,... | collective-permute-start | bytes 294920 | tf_op jit(solution)/shard_map/ppermute | solution.py:36
  195.4 6.3 %collective-permute-done.5 = f32[256,96]{0,1:T(8,128)S(1)} collective-permute-done((f32[256,96]{0,1:T(8,128)S(1)}, f32[256,96]{0,1:T(8,128)S(1)}, u32[]{:S(2)}, u32[]{:S(2)}) %collective-permute-start.5) | collective-permute-done | bytes 98336 | tf_op jit(solution)/shard_map/ppermute | solution.py:36
  201.7 0.7 add_bitcast_fusion
  (134 shorter events, 7.6 us)
Async XLA Ops:
  0.6 48.4 %copy-start = (bf16[8,1,128,128]{3,2,1,0:T(8,128)(2,1)S(1)}, bf16[8,1,128,128]{3,2,1,0:T(8,128)(2,1)}, u32[]{:S(2)}) copy-start(bf16[8,1,128,128]{3,2,1,0:T(8,128)(2,1)} %param.30) | copy-start | bytes 786436
  0.6 11.8 %copy-start.12 = (s32[32]{0:T(128)S(1)}, s32[32]{0:T(128)}, u32[]{:S(2)}) copy-start(s32[32]{0:T(128)} %param.35) | copy-start | bytes 388
  0.7 12.0 %copy-start.14 = (s32[8]{0:T(128)S(1)}, s32[8]{0:T(128)}, u32[]{:S(2)}) copy-start(s32[8]{0:T(128)} %param.37) | copy-start | bytes 100
  0.7 12.0 %copy-start.15 = (s32[1,8]{1,0:T(1,128)S(1)}, s32[1,8]{1,0:T(1,128)}, u32[]{:S(2)}) copy-start(s32[1,8]{1,0:T(1,128)} %param.34) | copy-start | bytes 100
  0.7 12.1 %copy-start.6 = (bf16[8,1,127,128]{3,0,2,1:T(8,128)(2,1)S(1)}, bf16[8,1,127,128]{3,0,2,1:T(8,128)(2,1)}, u32[]{:S(2)}) copy-start(bf16[8,1,127,128]{3,0,2,1:T(8,128)(2,1)} %param.32) | copy-start | bytes 780292
  0.7 12.1 %copy-start.7 = (bf16[8,1,127,128]{3,0,2,1:T(8,128)(2,1)S(1)}, bf16[8,1,127,128]{3,0,2,1:T(8,128)(2,1)}, u32[]{:S(2)}) copy-start(bf16[8,1,127,128]{3,0,2,1:T(8,128)(2,1)} %param.33) | copy-start | bytes 780292
  2.7 10.4 %copy-start.16 = (s32[5]{0:T(128)S(1)}, s32[5]{0:T(128)}, u32[]{:S(2)}) copy-start(s32[5]{0:T(128)} %param.36) | copy-start | bytes 64
  4.8 20.9 %all-to-all-start = ((f32[32,8,641]{2,1,0:T(8,128)}), f32[32,8,641]{2,1,0:T(8,128)S(1)}, u32[]{:S(2)}, u32[]{:S(2)}) async-start(f32[32,8,641]{2,1,0:T(8,128)} %pad_maximum_fusion.1), calls=%async_computation | async-start | bytes 1572864 | tf_op jit(solution)/shard_map/all_to_all | solution.py:51
  54.7 9.7 %copy-start.1 = (bf16[8,1,128,128]{3,2,0,1:T(8,128)(2,1)S(1)}, bf16[8,1,128,128]{3,2,0,1:T(8,128)(2,1)}, u32[]{:S(2)}) copy-start(bf16[8,1,128,128]{3,2,0,1:T(8,128)(2,1)} %get-tuple-element.68) | copy-start | bytes 786436
  55.4 9.6 %copy-start.4 = (bf16[8,1,128,128]{3,2,0,1:T(8,128)(2,1)S(1)}, bf16[8,1,128,128]{3,2,0,1:T(8,128)(2,1)}, u32[]{:S(2)}) copy-start(bf16[8,1,128,128]{3,2,0,1:T(8,128)(2,1)} %get-tuple-element.69) | copy-start | bytes 786436
  58.5 44.1 %copy-start.11 = (bf16[384,96]{0,1:T(8,128)(2,1)S(1)}, bf16[384,96]{0,1:T(8,128)(2,1)}, u32[]{:S(2)}) copy-start(bf16[384,96]{0,1:T(8,128)(2,1)} %param.25) | copy-start | bytes 221188
  58.5 67.7 %copy-start.3 = (bf16[1,256,96]{1,2,0:T(8,128)(2,1)S(1)}, bf16[1,256,96]{1,2,0:T(8,128)(2,1)}, u32[]{:S(2)}) copy-start(bf16[1,256,96]{1,2,0:T(8,128)(2,1)} %param.22) | copy-start | bytes 147460
  58.5 68.0 %copy-start.8 = (bf16[96,1024]{1,0:T(8,128)(2,1)S(1)}, bf16[96,1024]{1,0:T(8,128)(2,1)}, u32[]{:S(2)}) copy-start(bf16[96,1024]{1,0:T(8,128)(2,1)} %param.28) | copy-start | bytes 589828
  58.5 68.0 %copy-start.9 = (bf16[96,1024]{1,0:T(8,128)(2,1)S(1)}, bf16[96,1024]{1,0:T(8,128)(2,1)}, u32[]{:S(2)}) copy-start(bf16[96,1024]{1,0:T(8,128)(2,1)} %param.27) | copy-start | bytes 589828
  58.5 68.0 %copy-start.13 = (f32[96]{0:T(128)S(1)}, f32[96]{0:T(128)}, u32[]{:S(2)}) copy-start(f32[96]{0:T(128)} %param.26) | copy-start | bytes 1156
  58.5 19.0 %all-to-all-start.1 = ((f32[32,8,1,3,130]{4,1,3,2,0:T(8,128)}), f32[32,8,1,3,130]{4,1,3,2,0:T(8,128)S(1)}, u32[]{:S(2)}, u32[]{:S(2)}) async-start(f32[32,8,1,3,130]{4,1,3,2,0:T(8,128)} %maximum_bitcast_fusion), calls=%async_computation.1 | async-start | bytes 1572864 | tf_op jit(solution)/shard_map/all_to_all | solution.py:169
  64.5 62.5 %copy-start.2 = (bf16[8,1,128,128]{3,2,0,1:T(8,128)(2,1)}, bf16[8,1,128,128]{3,2,0,1:T(8,128)(2,1)S(1)}, u32[]{:S(2)}) copy-start(bf16[8,1,128,128]{3,2,0,1:T(8,128)(2,1)S(1)} %scatter.6) | copy-start | bytes 786436
  65.0 62.0 %copy-start.5 = (bf16[8,1,128,128]{3,2,0,1:T(8,128)(2,1)}, bf16[8,1,128,128]{3,2,0,1:T(8,128)(2,1)S(1)}, u32[]{:S(2)}) copy-start(bf16[8,1,128,128]{3,2,0,1:T(8,128)(2,1)S(1)} %scatter.9) | copy-start | bytes 786436
  102.8 5.3 %collective-permute-start = (f32[256,96]{0,1:T(8,128)S(1)}, f32[256,96]{0,1:T(8,128)S(1)}, u32[]{:S(2)}, u32[]{:S(2)}) collective-permute-start(f32[256,96]{0,1:T(8,128)S(1)} %fusion.65), channel_id=1, source_target_pairs={{0,32},{32,0},{64,96},{96,64},{128,160},{160,128},{192,224},{224,1... | collective-permute-start | bytes 294920 | tf_op jit(solution)/shard_map/ppermute | solution.py:36
  108.1 8.1 %collective-permute-start.1 = (f32[256,96]{0,1:T(8,128)S(1)}, f32[256,96]{0,1:T(8,128)S(1)}, u32[]{:S(2)}, u32[]{:S(2)}) collective-permute-start(f32[256,96]{0,1:T(8,128)S(1)} %add.109), channel_id=1, source_target_pairs={{0,64},{32,96},{64,0},{96,32},{128,192},{160,224},{192,128},{224,1... | collective-permute-start | bytes 294920 | tf_op jit(solution)/shard_map/ppermute | solution.py:36
  116.3 9.9 %collective-permute-start.2 = (f32[256,96]{0,1:T(8,128)S(1)}, f32[256,96]{0,1:T(8,128)S(1)}, u32[]{:S(2)}, u32[]{:S(2)}) collective-permute-start(f32[256,96]{0,1:T(8,128)S(1)} %add.110), channel_id=1, source_target_pairs={{0,128},{32,160},{64,192},{96,224},{128,0},{160,32},{192,64},{224,... | collective-permute-start | bytes 294920 | tf_op jit(solution)/shard_map/ppermute | solution.py:36
  161.6 15.8 %copy-start.10 = (bf16[1024,96]{0,1:T(8,128)(2,1)S(1)}, bf16[1024,96]{0,1:T(8,128)(2,1)}, u32[]{:S(2)}) copy-start(bf16[1024,96]{0,1:T(8,128)(2,1)} %param.29) | copy-start | bytes 589828
  177.8 5.2 %collective-permute-start.3 = (f32[256,96]{0,1:T(8,128)S(1)}, f32[256,96]{0,1:T(8,128)S(1)}, u32[]{:S(2)}, u32[]{:S(2)}) collective-permute-start(f32[256,96]{0,1:T(8,128)S(1)} %fusion.11), channel_id=1, source_target_pairs={{0,32},{32,0},{64,96},{96,64},{128,160},{160,128},{192,224},{224,1... | collective-permute-start | bytes 294920 | tf_op jit(solution)/shard_map/ppermute | solution.py:36
  183.0 8.1 %collective-permute-start.4 = (f32[256,96]{0,1:T(8,128)S(1)}, f32[256,96]{0,1:T(8,128)S(1)}, u32[]{:S(2)}, u32[]{:S(2)}) collective-permute-start(f32[256,96]{0,1:T(8,128)S(1)} %add.115), channel_id=1, source_target_pairs={{0,64},{32,96},{64,0},{96,32},{128,192},{160,224},{192,128},{224,1... | collective-permute-start | bytes 294920 | tf_op jit(solution)/shard_map/ppermute | solution.py:36
  191.1 10.6 %collective-permute-start.5 = (f32[256,96]{0,1:T(8,128)S(1)}, f32[256,96]{0,1:T(8,128)S(1)}, u32[]{:S(2)}, u32[]{:S(2)}) collective-permute-start(f32[256,96]{0,1:T(8,128)S(1)} %add.116), channel_id=1, source_target_pairs={{0,128},{32,160},{64,192},{96,224},{128,0},{160,32},{192,64},{224,... | collective-permute-start | bytes 294920 | tf_op jit(solution)/shard_map/ppermute | solution.py:36
